TPU v7x, 256 devices: a whole 4x4x8 slice. The times are simulated.
256 devices in a mesh: pipe: 2 (over core), expert: 128 (over x, z, y).
Axes of the slice: x: 4, y: 4, z: 8, core: 2. Of those that a mesh axis runs over, the one named last changes fastest.
Arguments:
- section_inputs: bfloat16 [2, 16384, 7168], P('pipe', 'expert'), may hold values from -6 to 6
- output_grads: bfloat16 [2, 16384, 7168], P('pipe', 'expert'), may hold values from -6 to 6
- w_gate: bfloat16 [2, 7168, 16384], P('pipe', None, 'expert'), may hold values from -0.0625 to 0.0625
- w_up: bfloat16 [2, 7168, 16384], P('pipe', None, 'expert'), may hold values from -0.0625 to 0.0625
- w_down: bfloat16 [2, 16384, 7168], P('pipe', 'expert'), may hold values from -0.125 to 0.125
- route_ids: int32 [2, 16384, 8], P('pipe', 'expert'), may hold values from 0 to 255, all different within a row; in each aligned block of 128 rows (0 to 127, 128 to 255, ..., all dimensions but the last counted through in order) at most 5 rows name the same one
- route_gates: float32 [2, 16384, 8], P('pipe', 'expert'), may hold values from 0.25 to 1
Outputs:
- handed_grads: bfloat16 [2, 16384, 7168], P('pipe', 'expert')
- down_grads: bfloat16 [2, 16384, 7168], P('pipe', 'expert')
Inputs may be any that keep to these rules, and one draw needn't show every extreme that they name: `route_ids`: each row names 8 different experts. Within the 128 rows of one device of one section, no expert is named by more than 5 rows.
All inputs are finite; a program needn't handle non-finite values.
Results may differ from a plain program's by a relative error of at most 0.0057.
Values may be sent and summed in bfloat16 or wider, within the bound.
No kernel may reach another device: no remote copies, remote signals or barrier semaphores. Data moves between devices by JAX's collectives and lax.ppermute only.
A program may use at most 192 MiB of HBM per device.

v0:
```python
import jax
import jax.numpy as jnp
from jax import lax
from jax.sharding import Mesh
from jax.sharding import PartitionSpec as P

SHARDS = 16
CAP = 5
TILE_ROWS = 16


def from_behind(value, axis, steps):
    count = lax.axis_size(axis)
    pairs = [(source, (source + steps) % count) for source in range(count)]
    return lax.ppermute(value, axis, pairs)


def body(section_inputs, output_grads, w_gate, w_up, w_down, route_ids, route_gates):
    inputs = section_inputs[0]
    grads = output_grads[0]
    route = route_ids[0]
    gate = route_gates[0]
    gate_cols = w_gate[0]
    up_cols = w_up[0]
    down_rows = w_down[0]
    tok_rows, model_width = inputs.shape
    block_width = gate_cols.shape[1]
    live_count = lax.axis_size("group")
    slot_count = CAP
    expert_ids = jnp.arange(live_count, dtype=jnp.int32)
    hit = route[:, :, None] == expert_ids
    member = jnp.sum(hit.astype(jnp.int32), axis=1)
    weight = jnp.sum(jnp.where(hit, gate[:, :, None], 0.0), axis=1)
    position = jnp.cumsum(member, axis=0) - member
    slot_ids = jnp.arange(slot_count, dtype=jnp.int32)
    pick = (member[:, :, None] == 1) & (position[:, :, None] == slot_ids)
    pick_mat = pick.astype(jnp.bfloat16).reshape(tok_rows, live_count * slot_count)
    rows_first = (((0,), (0,)), ((), ()))
    rows_in = lax.dot_general(
        pick_mat, inputs, rows_first, preferred_element_type=jnp.float32
    ).astype(jnp.bfloat16)
    chosen_grads = lax.dot_general(pick_mat, grads, rows_first, preferred_element_type=jnp.float32)
    slot_gate = jnp.sum(pick.astype(jnp.float32) * weight[:, :, None], axis=0).reshape(
        live_count * slot_count, 1
    )
    rows_grad = (chosen_grads * slot_gate).astype(jnp.bfloat16)
    send_in = rows_in.reshape(live_count, TILE_ROWS, -1)
    send_grad = rows_grad.reshape(live_count, TILE_ROWS, -1)
    near_rows = live_count * slot_count
    near_in = lax.all_to_all(send_in, "group", 0, 0, tiled=True).reshape(near_rows, model_width)
    near_grad = lax.all_to_all(send_grad, "group", 0, 0, tiled=True).reshape(near_rows, model_width)
    got_in = lax.all_gather(near_in, "member", axis=0, tiled=True)
    got_grad = lax.all_gather(near_grad, "member", axis=0, tiled=True)
    both_cols = jnp.concatenate([gate_cols, up_cols], axis=1)
    both_cols, got_in, got_grad = lax.optimization_barrier((both_cols, got_in, got_grad))
    both_slice = lax.all_to_all(
        both_cols.reshape(SHARDS, -1, both_cols.shape[1]), "member", 0, 0, tiled=True
    )
    members = lax.axis_size("member")
    groups = live_count
    gate_pre = jnp.dot(got_in, gate_cols, preferred_element_type=jnp.float32)
    up_pre = jnp.dot(got_in, up_cols, preferred_element_type=jnp.float32)
    sigma = jax.nn.sigmoid(gate_pre)
    silu_gate = gate_pre * sigma
    hidden = (silu_gate * up_pre).astype(jnp.bfloat16)
    contract = (((1,), (1,)), ((), ()))
    back_hidden = lax.dot_general(got_grad, down_rows, contract, preferred_element_type=jnp.float32)
    grad_gate = (back_hidden * up_pre * sigma * (1.0 + gate_pre * (1.0 - sigma))).astype(
        jnp.bfloat16
    )
    grad_up = (back_hidden * silu_gate).astype(jnp.bfloat16)
    both_grad = jnp.concatenate([grad_gate, grad_up], axis=1).T
    down_part = lax.dot_general(
        hidden, got_grad, rows_first, preferred_element_type=jnp.float32
    ).astype(jnp.bfloat16)
    both_slice, both_grad, down_part = lax.optimization_barrier((both_slice, both_grad, down_part))
    all_grad = lax.all_gather(both_grad, "member", axis=0, tiled=False)
    slice_value = lax.dot_general(
        all_grad, both_slice, (((0, 1), (0, 2)), ((), ())), preferred_element_type=jnp.float32
    )
    slice_width = slice_value.shape[1]
    slice_value = slice_value.reshape(members, groups, slot_count, slice_width)
    slice_value = jnp.transpose(slice_value, (1, 0, 2, 3)).reshape(
        groups * members, slot_count, slice_width
    )
    back = lax.all_to_all(slice_value.astype(jnp.bfloat16), ("group", "member"), 0, 0, tiled=True)
    back = back.reshape(groups, members, slot_count, slice_width)
    returned = jnp.transpose(back, (0, 2, 1, 3)).reshape(groups * slot_count, model_width)
    other_grads = from_behind(grads, "pipe", -1)
    other_pick = from_behind(pick_mat, "pipe", -1)
    other_returned = from_behind(returned, "pipe", -1)
    branch = jnp.dot(other_pick, other_returned, preferred_element_type=jnp.float32)
    handed = (other_grads.astype(jnp.float32) + branch).astype(jnp.bfloat16)
    return (handed[None], down_part[None])


def solution(mesh):
    pipe = mesh.shape["pipe"]
    width = mesh.shape["expert"]
    groups = width // SHARDS
    inner = Mesh(mesh.devices.reshape(pipe, groups, SHARDS), ("pipe", "group", "member"))
    rows = P("pipe", ("group", "member"), None)
    cols = P("pipe", None, ("group", "member"))
    return jax.shard_map(
        body,
        mesh=inner,
        in_specs=(rows, rows, cols, cols, rows, rows, rows),
        out_specs=(rows, rows),
        check_vma=False,
    )
```

profile of v0, /device:TPU:1, one launch (start us, length us, event | category | flops | bytes accessed | tf_op | source)
XLA Modules:
  0.0 497.3 jit_solution(12213174864542856389)
XLA Ops:
  7.2 0.8 convert_reduce_fusion
  9.3 1.9 fusion
  11.2 1.0 reshape.113
  12.2 26.1 %all_to_all.20 = bf16[8,16,2240]{2,1,0:T(8,128)(2,1)S(1)} all-to-all(bf16[8,16,2240]{2,1,0:T(8,128)(2,1)S(1)} %reshape.113), channel_id=1, replica_groups=mesh['pipe'=2,'group'=8,'member'=16] {'group'}, dimensions={0} | all-to-all | bytes 1146880 | tf_op jit(solution)/shard_map/all_to_all | solution.py:51
  38.3 1.7 reshape.114
  40.5 1.0 reshape.111
  41.5 14.6 %all_to_all.21 = bf16[8,16,2240]{2,1,0:T(8,128)(2,1)S(1)} all-to-all(bf16[8,16,2240]{2,1,0:T(8,128)(2,1)S(1)} %reshape.111), channel_id=1, replica_groups=mesh['pipe'=2,'group'=8,'member'=16] {'group'}, dimensions={0} | all-to-all | bytes 1146880 | tf_op jit(solution)/shard_map/all_to_all | solution.py:50
  56.1 1.7 reshape.112
  57.9 4.3 pad_maximum_fusion
  62.2 96.5 %all-gather.7.cloned.1.call-done = bf16[640,7168]{1,0:T(8,128)(2,1)} async-done(((bf16[40,7168]{1,0:T(8,128)(2,1)}), bf16[640,7168]{1,0:T(8,128)(2,1)}) %all-gather.7.cloned.1.call-update) | async-done | bytes 9175056 | tf_op jit(solution)/shard_map/all_gather | solution.py:53
  158.7 109.4 %all-gather.5.cloned.1.call-done = bf16[640,7168]{1,0:T(8,128)(2,1)} async-done(((bf16[40,7168]{1,0:T(8,128)(2,1)}), bf16[640,7168]{1,0:T(8,128)(2,1)}) %all-gather.5.cloned.1.call-update) | async-done | bytes 9175056 | tf_op jit(solution)/shard_map/all_gather | solution.py:52
  268.1 4.5 all-to-all-start.2
  272.9 7.0 %fusion.9 = f32[640,128]{0,1:T(8,128)S(1)} fusion(bf16[640,7168]{1,0:T(8,128)(2,1)} %all-gather.5.cloned.1.call-done, bf16[1,7168,128]{2,1,0:T(8,128)(2,1)} %param.10), kind=kOutput, calls=%fused_computation.27 | convolution fusion | flops 1174405120 | bytes 11337728 | tf_op jit(solution)/shard_map/dot_general | solution.py:62
  280.0 6.7 %fusion.2 = f32[640,128]{0,1:T(8,128)S(1)} fusion(bf16[640,7168]{1,0:T(8,128)(2,1)} %all-gather.7.cloned.1.call-done, bf16[1,128,7168]{2,1,0:T(8,128)(2,1)S(1)} %copy-done.2), kind=kOutput, calls=%fused_computation.7 | convolution fusion | flops 1174405120 | bytes 11337728 | tf_op jit(solution)/shard_map/dot_general | solution.py:67
  286.7 3.0 multiply_convert_fusion.2
  290.5 6.5 %convolution_convert_fusion = bf16[128,7168]{1,0:T(8,128)(2,1)} fusion(bf16[640,7168]{1,0:T(8,128)(2,1)} %all-gather.7.cloned.1.call-done, f32[640,128]{0,1:T(8,128)S(1)} %fusion.9, f32[640,128]{0,1:T(8,128)S(1)} %get-tuple-element.16), kind=kOutput, calls=%fused_computation | convolution fusion | flops 1175814144 | bytes 11665408 | tf_op jit(solution)/shard_map/dot_general | solution.py:73
  296.9 44.8 %all-to-all-done.2 = bf16[16,448,256]{2,1,0:T(8,128)(2,1)} async-done(((bf16[16,448,256]{2,1,0:T(8,128)(2,1)}), bf16[16,448,256]{2,1,0:T(8,128)(2,1)}, u32[]{:S(2)}, u32[]{:S(2)}) %all-to-all-start.2) | async-done | bytes 3670048 | tf_op jit(solution)/shard_map/all_to_all | solution.py:56
  341.7 2.8 collective-permute-start
  344.5 91.1 %all-gather.9.cloned.1.call-done = bf16[4096,640]{1,0:T(8,128)(2,1)} async-done(((bf16[256,640]{1,0:T(8,128)(2,1)}), bf16[4096,640]{1,0:T(8,128)(2,1)}) %all-gather.9.cloned.1.call-update) | async-done | bytes 5242896 | tf_op jit(solution)/shard_map/all_gather | solution.py:77
  435.7 6.6 %fusion.5 = bf16[640,448]{0,1:T(8,128)(2,1)S(1)} fusion(bf16[16,448,256]{2,1,0:T(8,128)(2,1)} %all-to-all-done.2, bf16[16,256,640]{2,1,0:T(8,128)(2,1)} %bitcast.68), kind=kOutput, calls=%fused_computation.11 | convolution fusion | flops 2349096960 | bytes 9486336 | tf_op jit(solution)/shard_map/dot_general | solution.py:78
  443.6 28.7 %all_to_all.22 = bf16[128,5,448]{2,1,0:T(8,128)(2,1)S(1)} all-to-all(bf16[128,5,448]{2,1,0:T(8,128)(2,1)S(1)} %copy.31), channel_id=1, replica_groups=mesh['pipe'=2,'group'=8,'member'=16] {'group','member'}, dimensions={0} | all-to-all | bytes 1146880 | tf_op jit(solution)/shard_map/all_to_all | solution.py:86
  473.3 12.4 %collective-permute-start.2 = (bf16[40,7168]{1,0:T(8,128)(2,1)S(1)}, bf16[40,7168]{1,0:T(8,128)(2,1)S(1)}, u32[]{:S(2)}, u32[]{:S(2)}) collective-permute-start(bf16[40,7168]{1,0:T(8,128)(2,1)S(1)} %reshape.117), channel_id=1, source_target_pairs={{0,128},{128,0},{1,129},{129,1},{2,130},{130,2},{3,131},{131,3},{4... | collective-permute-start | bytes 1720328 | tf_op jit(solution)/shard_map/ppermute | solution.py:15
  486.0 1.3 collective-permute-done.1
  487.3 3.4 fusion.1
  (47 shorter events, 5.4 us)
Async XLA Ops:
  7.2 32.9 %copy-start = (bf16[1,128,7168]{2,1,0:T(8,128)(2,1)S(1)}, bf16[1,128,7168]{2,1,0:T(8,128)(2,1)}, u32[]{:S(2)}) copy-start(bf16[1,128,7168]{2,1,0:T(8,128)(2,1)} %param.7) | copy-start | bytes 5505028
  7.2 151.5 %all-gather.7.cloned.1.call-start = ((), (), s32[]{:S(2)}) async-start(), calls=%async_computation.5 | async-start | bytes 9748480 | tf_op jit(solution)/shard_map/all_gather | solution.py:53
  40.0 228.1 %all-gather.5.cloned.1.call-start = ((), (), s32[]{:S(2)}) async-start(), calls=%async_computation.4 | async-start | bytes 9748480 | tf_op jit(solution)/shard_map/all_gather | solution.py:52
  268.1 73.6 %all-to-all-start.2 = ((bf16[16,448,256]{2,1,0:T(8,128)(2,1)}), bf16[16,448,256]{2,1,0:T(8,128)(2,1)}, u32[]{:S(2)}, u32[]{:S(2)}) async-start(bf16[16,448,256]{2,1,0:T(8,128)(2,1)} %bitcast.56), calls=%async_computation.2 | async-start | bytes 7340032 | tf_op jit(solution)/shard_map/all_to_all | solution.py:56
  272.6 163.0 %all-gather.9.cloned.1.call-start = ((), (), s32[]{:S(2)}) async-start(), calls=%async_computation.6 | async-start | bytes 5570560 | tf_op jit(solution)/shard_map/all_gather | solution.py:77
  272.9 7.1 %copy-start.2 = (bf16[1,128,7168]{2,1,0:T(8,128)(2,1)S(1)}, bf16[1,128,7168]{2,1,0:T(8,128)(2,1)}, u32[]{:S(2)}) copy-start(bf16[1,128,7168]{2,1,0:T(8,128)(2,1)} %param.11) | copy-start | bytes 5505028
  272.9 13.8 %slice-start = ((s8[9175040]{0:T(1024)(128)(4,1)}), s8[4194304]{0:T(1024)(128)(4,1)S(1)}, s32[]{:S(2)}) async-start(s8[9175040]{0:T(1024)(128)(4,1)} %bitcast.54), calls=%async_computation.7 | async-start | bytes 8388608
  272.9 13.8 %slice-start.1 = ((s8[9175040]{0:T(1024)(128)(4,1)}), s8[4194304]{0:T(1024)(128)(4,1)S(1)}, s32[]{:S(2)}) async-start(s8[9175040]{0:T(1024)(128)(4,1)} %bitcast.54), calls=%async_computation.8 | async-start | bytes 8388608
  280.0 6.7 %slice-start.2 = ((s8[9175040]{0:T(1024)(128)(4,1)}), s8[786432]{0:T(1024)(128)(4,1)S(1)}, s32[]{:S(2)}) async-start(s8[9175040]{0:T(1024)(128)(4,1)} %bitcast.54), calls=%async_computation.9 | async-start | bytes 1572864
  280.0 6.7 %copy-start.1 = (bf16[1,7168,128]{2,1,0:T(8,128)(2,1)S(1)}, bf16[1,7168,128]{2,1,0:T(8,128)(2,1)}, u32[]{:S(2)}) copy-start(bf16[1,7168,128]{2,1,0:T(8,128)(2,1)} %param.9) | copy-start | bytes 5505028
  341.7 145.6 %collective-permute-start = (bf16[128,7168]{1,0:T(8,128)(2,1)}, bf16[128,7168]{1,0:T(8,128)(2,1)}, u32[]{:S(2)}, u32[]{:S(2)}) collective-permute-start(bf16[128,7168]{1,0:T(8,128)(2,1)} %bitcast.63), channel_id=1, source_target_pairs={{0,128},{128,0},{1,129},{129,1},{2,130},{130,2},{3,131},{131,3},{4... | collective-permute-start | bytes 5505032 | tf_op jit(solution)/shard_map/ppermute | solution.py:15
  473.3 14.0 %collective-permute-start.2 = (bf16[40,7168]{1,0:T(8,128)(2,1)S(1)}, bf16[40,7168]{1,0:T(8,128)(2,1)S(1)}, u32[]{:S(2)}, u32[]{:S(2)}) collective-permute-start(bf16[40,7168]{1,0:T(8,128)(2,1)S(1)} %reshape.117), channel_id=1, source_target_pairs={{0,128},{128,0},{1,129},{129,1},{2,130},{130,2},{3,131},{131,3},{4... | collective-permute-start | bytes 1720328 | tf_op jit(solution)/shard_map/ppermute | solution.py:15
  485.9 1.4 collective-permute-start.1
Sparse Core Ops, SparseCore 0:
  40.2 118.4 all-gather.6
  161.0 107.0 all-gather.4
  341.9 93.7 all-gather.8
where the time goes:
time: 498 us; the launch traced here: 497 us
  waiting for transfers between devices  343 us (69%)
  blocking collectives  69.4 us (14%)
  matrix products  35.4 us (7%)
  starting transfers between devices  20 us (4%)
  between operations  14 us (3%)
  local copies, waits for them, and re-layouts  8.14 us (2%)
  other arithmetic  7.01 us (1%)
    all_gather x1, waiting for transfers between devices, body(): got_in = lax.all_gather(near_in, 'member', axis=0, tiled=True)  109 us
    all_gather x1, waiting for transfers between devices, body(): got_grad = lax.all_gather(near_grad, 'member', axis=0, tiled=True)  96.5 us
    all_gather x1, waiting for transfers between devices, body(): all_grad = lax.all_gather(both_grad, 'member', axis=0, tiled=False)  91.1 us
    all_to_all x1, waiting for transfers between devices, body(): lax.all_to_all(both_cols.reshape(SHARDS, -1, both_cols.shape[1]), 'member...  44.8 us
    all_to_all x1, blocking collectives, body(): lax.all_to_all(slice_value.astype(jnp.bfloat16), ('group', 'member'), 0,...  28.7 us
    all_to_all x1, blocking collectives, body(): lax.all_to_all(send_grad, 'group', 0, 0, tiled=True)  26.1 us
    ppermute x3, starting transfers between devices, from_behind(): return lax.ppermute(value, axis, pairs)  15.2 us
    all_to_all x1, blocking collectives, body(): lax.all_to_all(send_in, 'group', 0, 0, tiled=True)  14.6 us
  transfers between devices with their start and end apart: 7, of which 5 were waited for; matrix products, arithmetic and copies ran while one was open for 8% of the time, Pallas kernels for 0%

commit v1 on v0

--- a/solution.py
+++ b/solution.py
@@ -49,7 +49,8 @@
     near_rows = live_count * slot_count
     near_in = lax.all_to_all(send_in, "group", 0, 0, tiled=True).reshape(near_rows, model_width)
     near_grad = lax.all_to_all(send_grad, "group", 0, 0, tiled=True).reshape(near_rows, model_width)
-    got_in = lax.all_gather(near_in, "member", axis=0, tiled=True)
+    outgoing = jnp.stack([near_in] * lax.axis_size("member"))
+    got_in = jnp.concatenate(lax.all_to_all(outgoing, "member", 0, 0), axis=0)
     got_grad = lax.all_gather(near_grad, "member", axis=0, tiled=True)
     both_cols = jnp.concatenate([gate_cols, up_cols], axis=1)
     both_cols, got_in, got_grad = lax.optimization_barrier((both_cols, got_in, got_grad))

time: 498 us -> 595 us (1.19)
  waiting for transfers between devices: 343 us -> 411 us
  starting transfers between devices: 20 us -> 85.7 us
  blocking collectives: 69.4 us -> 28.7 us
    all_gather x1, waiting for transfers between devices: 96.5 us -> 220 us  [body(): got_grad = lax.all_gather(near_grad, 'member', axis=0, tiled=True)]
    all_gather x1 -> x0, waiting for transfers between devices: 109 us -> none  [body(): got_in = lax.all_gather(near_in, 'member', axis=0, tiled=True)]
    all_to_all x0 -> x3, waiting for transfers between devices: none -> 50.9 us  [the longest x1 27.8 us: body(): got_in = jnp.concatenate(lax.all_to_all(outgoing, 'member', 0, 0), axis=0)]
    all_to_all x2 -> x0, blocking collectives: 40.7 us -> none  [the longest x1 26.1 us: body(): lax.all_to_all(send_grad, 'group', 0, 0, tiled=True)]
    all_to_all x1, starting transfers between devices: 4.52 us -> 39.5 us  [body(): lax.all_to_all(both_cols.reshape(SHARDS, -1, both_cols.shape[1]), 'member...]
    all_to_all x0 -> x3, starting transfers between devices: none -> 30.7 us  [the longest x1 15.6 us: body(): got_in = jnp.concatenate(lax.all_to_all(outgoing, 'member', 0, 0), axis=0)]
  transfers between devices with their start and end apart: 7 -> 9, of which waited for: 5 -> 7; matrix products, arithmetic and copies ran while one was open for 8% -> 8% of each run, Pallas kernels for 0% -> 0%
where the time goes in v1:
time: 595 us
  waiting for transfers between devices  411 us (69%)
  starting transfers between devices  85.7 us (14%)
  matrix products  34.7 us (6%)
  blocking collectives  28.7 us (5%)
  between operations  14.2 us (2%)
  local copies, waits for them, and re-layouts  13.8 us (2%)
  other arithmetic  6.51 us (1%)
    all_gather x1, waiting for transfers between devices, body(): got_grad = lax.all_gather(near_grad, 'member', axis=0, tiled=True)  220 us
    all_gather x1, waiting for transfers between devices, body(): all_grad = lax.all_gather(both_grad, 'member', axis=0, tiled=False)  93.8 us
    all_to_all x1, waiting for transfers between devices, body(): lax.all_to_all(both_cols.reshape(SHARDS, -1, both_cols.shape[1]), 'member...  45.5 us
    all_to_all x1, starting transfers between devices, body(): lax.all_to_all(both_cols.reshape(SHARDS, -1, both_cols.shape[1]), 'member...  39.5 us
    all_to_all x1, blocking collectives, body(): lax.all_to_all(slice_value.astype(jnp.bfloat16), ('group', 'member'), 0,...  28.7 us
    all_to_all x1, waiting for transfers between devices, body(): got_in = jnp.concatenate(lax.all_to_all(outgoing, 'member', 0, 0), axis=0)  27.8 us
    all_to_all x1, starting transfers between devices, body(): got_in = jnp.concatenate(lax.all_to_all(outgoing, 'member', 0, 0), axis=0)  15.6 us
    ppermute x3, starting transfers between devices, from_behind(): return lax.ppermute(value, axis, pairs)  15.3 us
  transfers between devices with their start and end apart: 9, of which 7 were waited for; matrix products, arithmetic and copies ran while one was open for 8% of the time, Pallas kernels for 0%

profile of v1, /device:TPU:1, one launch (start us, length us, event | category | flops | bytes accessed | tf_op | source)
XLA Modules:
  0.0 594.9 jit_solution(7887377844739609826)
XLA Ops:
  9.3 1.9 fusion
  11.2 1.8 reshape.115
  13.0 11.5 %all-to-all-start.2 = ((bf16[8,16,2240]{2,1,0:T(8,128)(2,1)}), bf16[8,16,2240]{2,1,0:T(8,128)(2,1)S(1)}, u32[]{:S(2)}, u32[]{:S(2)}) async-start(bf16[8,16,2240]{2,1,0:T(8,128)(2,1)} %reshape.115), calls=%async_computation.2 | async-start | bytes 1179648 | tf_op jit(solution)/shard_map/all_to_all | solution.py:51
  24.9 1.8 reshape.113
  26.6 12.7 %all-to-all-done.2 = bf16[8,16,2240]{2,1,0:T(8,128)(2,1)S(1)} async-done(((bf16[8,16,2240]{2,1,0:T(8,128)(2,1)}), bf16[8,16,2240]{2,1,0:T(8,128)(2,1)S(1)}, u32[]{:S(2)}, u32[]{:S(2)}) %all-to-all-start.2) | async-done | bytes 573472 | tf_op jit(solution)/shard_map/all_to_all | solution.py:51
  39.3 3.5 all-to-all-start
  44.7 10.4 %all-to-all-done = bf16[8,16,2240]{2,1,0:T(8,128)(2,1)S(1)} async-done(((bf16[8,16,2240]{2,1,0:T(8,128)(2,1)}), bf16[8,16,2240]{2,1,0:T(8,128)(2,1)S(1)}, u32[]{:S(2)}, u32[]{:S(2)}) %all-to-all-start) | async-done | bytes 573472 | tf_op jit(solution)/shard_map/all_to_all | solution.py:50
  56.0 4.7 stack.3
  60.8 15.6 %all-to-all-start.1 = ((bf16[16,40,7168]{2,1,0:T(8,128)(2,1)}), bf16[16,40,7168]{2,1,0:T(8,128)(2,1)}, u32[]{:S(2)}, u32[]{:S(2)}) async-start(bf16[16,40,7168]{2,1,0:T(8,128)(2,1)} %stack.3), calls=%async_computation.1 | async-start | bytes 18350080 | tf_op jit(solution)/shard_map/all_to_all | solution.py:53
  76.4 3.8 pad_maximum_fusion
  80.2 219.6 %all-gather.4.cloned.1.call-done = bf16[640,7168]{1,0:T(8,128)(2,1)} async-done(((bf16[40,7168]{1,0:T(8,128)(2,1)}), bf16[640,7168]{1,0:T(8,128)(2,1)}) %all-gather.4.cloned.1.call-update) | async-done | bytes 9175056 | tf_op jit(solution)/shard_map/all_gather | solution.py:54
  299.9 27.8 %all-to-all-done.1 = bf16[16,40,7168]{2,1,0:T(8,128)(2,1)} async-done(((bf16[16,40,7168]{2,1,0:T(8,128)(2,1)}), bf16[16,40,7168]{2,1,0:T(8,128)(2,1)}, u32[]{:S(2)}, u32[]{:S(2)}) %all-to-all-start.1) | async-done | bytes 9175072 | tf_op jit(solution)/shard_map/all_to_all | solution.py:53
  327.6 39.5 %all-to-all-start.3 = ((bf16[16,448,256]{2,1,0:T(8,128)(2,1)}), bf16[16,448,256]{2,1,0:T(8,128)(2,1)}, u32[]{:S(2)}, u32[]{:S(2)}) async-start(bf16[16,448,256]{2,1,0:T(8,128)(2,1)} %bitcast.55), calls=%async_computation.3 | async-start | bytes 7340032 | tf_op jit(solution)/shard_map/all_to_all | solution.py:57
  367.4 6.5 %fusion.9 = f32[640,128]{0,1:T(8,128)S(1)} fusion(bf16[640,7168]{1,0:T(8,128)(2,1)} %bitcast.5, bf16[1,7168,128]{2,1,0:T(8,128)(2,1)S(1)} %copy-done.3), kind=kOutput, calls=%fused_computation.27 | convolution fusion | flops 1174405120 | bytes 11337728 | tf_op jit(solution)/shard_map/dot_general | solution.py:63
  374.1 2.9 fusion.2
  377.0 6.5 %multiply_convert_fusion.2 = (bf16[640,128]{0,1:T(8,128)(2,1)S(1)}, bf16[640,128]{0,1:T(8,128)(2,1)S(1)}, f32[640,128]{0,1:T(8,128)S(1)}) fusion(f32[640,128]{0,1:T(8,128)S(1)} %fusion.2, f32[640,128]{0,1:T(8,128)S(1)} %fusion.9, bf16[640,7168]{1,0:T(8,128)(2,1)} %bitcast.5, bf16[1,7168,128]{2,1,0:T(8,128)(2,1)S(1)} %copy-done.4), kind=kOutput, calls=%fused_computation.16 | convolution fusion | flops 1175470080 | bytes 12320768 | tf_op jit(solution)/shard_map/dot_general | solution.py:62
  384.3 6.5 %convolution_convert_fusion = bf16[128,7168]{1,0:T(8,128)(2,1)} fusion(bf16[640,7168]{1,0:T(8,128)(2,1)} %all-gather.4.cloned.1.call-done, f32[640,128]{0,1:T(8,128)S(1)} %fusion.9, f32[640,128]{0,1:T(8,128)S(1)} %get-tuple-element.16), kind=kOutput, calls=%fused_computation | convolution fusion | flops 1175814144 | bytes 11665408 | tf_op jit(solution)/shard_map/dot_general | solution.py:74
  390.7 45.5 %all-to-all-done.3 = bf16[16,448,256]{2,1,0:T(8,128)(2,1)} async-done(((bf16[16,448,256]{2,1,0:T(8,128)(2,1)}), bf16[16,448,256]{2,1,0:T(8,128)(2,1)}, u32[]{:S(2)}, u32[]{:S(2)}) %all-to-all-start.3) | async-done | bytes 3670048 | tf_op jit(solution)/shard_map/all_to_all | solution.py:57
  436.3 2.8 collective-permute-start
  439.1 93.8 %all-gather.6.cloned.1.call-done = bf16[4096,640]{1,0:T(8,128)(2,1)} async-done(((bf16[256,640]{1,0:T(8,128)(2,1)}), bf16[4096,640]{1,0:T(8,128)(2,1)}) %all-gather.6.cloned.1.call-update) | async-done | bytes 5242896 | tf_op jit(solution)/shard_map/all_gather | solution.py:78
  532.9 6.6 %fusion.5 = bf16[640,448]{0,1:T(8,128)(2,1)S(1)} fusion(bf16[16,448,256]{2,1,0:T(8,128)(2,1)} %all-to-all-done.3, bf16[16,256,640]{2,1,0:T(8,128)(2,1)} %bitcast.66), kind=kOutput, calls=%fused_computation.11 | convolution fusion | flops 2349096960 | bytes 9486336 | tf_op jit(solution)/shard_map/dot_general | solution.py:79
  540.9 28.7 %all_to_all.25 = bf16[128,5,448]{2,1,0:T(8,128)(2,1)S(1)} all-to-all(bf16[128,5,448]{2,1,0:T(8,128)(2,1)S(1)} %copy.31), channel_id=1, replica_groups=mesh['pipe'=2,'group'=8,'member'=16] {'group','member'}, dimensions={0} | all-to-all | bytes 1146880 | tf_op jit(solution)/shard_map/all_to_all | solution.py:87
  570.6 12.4 %collective-permute-start.2 = (bf16[40,7168]{1,0:T(8,128)(2,1)S(1)}, bf16[40,7168]{1,0:T(8,128)(2,1)S(1)}, u32[]{:S(2)}, u32[]{:S(2)}) collective-permute-start(bf16[40,7168]{1,0:T(8,128)(2,1)S(1)} %reshape.119), channel_id=1, source_target_pairs={{0,128},{128,0},{1,129},{129,1},{2,130},{130,2},{3,131},{131,3},{4... | collective-permute-start | bytes 1720328 | tf_op jit(solution)/shard_map/ppermute | solution.py:15
  584.6 3.4 fusion.1
  (48 shorter events, 10.3 us)
Async XLA Ops:
  7.2 17.3 %copy-start = (bf16[1,128,7168]{2,1,0:T(8,128)(2,1)S(1)}, bf16[1,128,7168]{2,1,0:T(8,128)(2,1)}, u32[]{:S(2)}) copy-start(bf16[1,128,7168]{2,1,0:T(8,128)(2,1)} %param.7) | copy-start | bytes 5505028
  13.0 26.4 %all-to-all-start.2 = ((bf16[8,16,2240]{2,1,0:T(8,128)(2,1)}), bf16[8,16,2240]{2,1,0:T(8,128)(2,1)S(1)}, u32[]{:S(2)}, u32[]{:S(2)}) async-start(bf16[8,16,2240]{2,1,0:T(8,128)(2,1)} %reshape.115), calls=%async_computation.2 | async-start | bytes 1179648 | tf_op jit(solution)/shard_map/all_to_all | solution.py:51
  39.3 15.8 %all-to-all-start = ((bf16[8,16,2240]{2,1,0:T(8,128)(2,1)}), bf16[8,16,2240]{2,1,0:T(8,128)(2,1)S(1)}, u32[]{:S(2)}, u32[]{:S(2)}) async-start(bf16[8,16,2240]{2,1,0:T(8,128)(2,1)} %reshape.113), calls=%async_computation | async-start | bytes 1179648 | tf_op jit(solution)/shard_map/all_to_all | solution.py:50
  42.9 257.0 %all-gather.4.cloned.1.call-start = ((), (), s32[]{:S(2)}) async-start(), calls=%async_computation.5 | async-start | bytes 9748480 | tf_op jit(solution)/shard_map/all_gather | solution.py:54
  60.8 15.7 %copy-start.3 = (bf16[1,7168,128]{2,1,0:T(8,128)(2,1)S(1)}, bf16[1,7168,128]{2,1,0:T(8,128)(2,1)}, u32[]{:S(2)}) copy-start(bf16[1,7168,128]{2,1,0:T(8,128)(2,1)} %param.10) | copy-start | bytes 5505028
  60.8 266.9 %all-to-all-start.1 = ((bf16[16,40,7168]{2,1,0:T(8,128)(2,1)}), bf16[16,40,7168]{2,1,0:T(8,128)(2,1)}, u32[]{:S(2)}, u32[]{:S(2)}) async-start(bf16[16,40,7168]{2,1,0:T(8,128)(2,1)} %stack.3), calls=%async_computation.1 | async-start | bytes 18350080 | tf_op jit(solution)/shard_map/all_to_all | solution.py:53
  327.6 108.6 %all-to-all-start.3 = ((bf16[16,448,256]{2,1,0:T(8,128)(2,1)}), bf16[16,448,256]{2,1,0:T(8,128)(2,1)}, u32[]{:S(2)}, u32[]{:S(2)}) async-start(bf16[16,448,256]{2,1,0:T(8,128)(2,1)} %bitcast.55), calls=%async_computation.3 | async-start | bytes 7340032 | tf_op jit(solution)/shard_map/all_to_all | solution.py:57
  367.1 165.8 %all-gather.6.cloned.1.call-start = ((), (), s32[]{:S(2)}) async-start(), calls=%async_computation.6 | async-start | bytes 5570560 | tf_op jit(solution)/shard_map/all_gather | solution.py:78
  367.4 6.6 %copy-start.2 = (bf16[640,7168]{1,0:T(8,128)(2,1)S(1)}, bf16[640,7168]{1,0:T(8,128)(2,1)}, u32[]{:S(2)}) copy-start(bf16[640,7168]{1,0:T(8,128)(2,1)} %all-gather.4.cloned.1.call-done) | copy-start | bytes 27525124
  367.4 6.7 %copy-start.5 = (bf16[1,128,7168]{2,1,0:T(8,128)(2,1)S(1)}, bf16[1,128,7168]{2,1,0:T(8,128)(2,1)}, u32[]{:S(2)}) copy-start(bf16[1,128,7168]{2,1,0:T(8,128)(2,1)} %param.11) | copy-start | bytes 5505028
  374.1 3.0 copy-start.4
  436.3 148.3 %collective-permute-start = (bf16[128,7168]{1,0:T(8,128)(2,1)}, bf16[128,7168]{1,0:T(8,128)(2,1)}, u32[]{:S(2)}, u32[]{:S(2)}) collective-permute-start(bf16[128,7168]{1,0:T(8,128)(2,1)} %bitcast), channel_id=1, source_target_pairs={{0,128},{128,0},{1,129},{129,1},{2,130},{130,2},{3,131},{131,3},{4... | collective-permute-start | bytes 5505032 | tf_op jit(solution)/shard_map/ppermute | solution.py:15
  569.6 18.4 %copy-start.1 = (bf16[1,128,7168]{2,1,0:T(8,128)(2,1)S(1)}, bf16[1,128,7168]{2,1,0:T(8,128)(2,1)}, u32[]{:S(2)}) copy-start(bf16[1,128,7168]{2,1,0:T(8,128)(2,1)} %param.7) | copy-start | bytes 5505028
  570.6 14.0 %collective-permute-start.2 = (bf16[40,7168]{1,0:T(8,128)(2,1)S(1)}, bf16[40,7168]{1,0:T(8,128)(2,1)S(1)}, u32[]{:S(2)}, u32[]{:S(2)}) collective-permute-start(bf16[40,7168]{1,0:T(8,128)(2,1)S(1)} %reshape.119), channel_id=1, source_target_pairs={{0,128},{128,0},{1,129},{129,1},{2,130},{130,2},{3,131},{131,3},{4... | collective-permute-start | bytes 1720328 | tf_op jit(solution)/shard_map/ppermute | solution.py:15
  583.2 1.4 collective-permute-start.1
Sparse Core Ops, SparseCore 0:
  46.1 253.7 all-gather.3
  436.4 96.4 all-gather.5
